TPU v7x, 32 devices: a whole 2x2x4 slice. The times are simulated.
32 devices in a mesh: region: 2 (over y), tile: 4 (over z), corner: 2 (over x), kern: 2 (over core).
Axes of the slice: x: 2, y: 2, z: 4, core: 2. Of those that a mesh axis runs over, the one named last changes fastest.
Arguments:
- tile_mask: bfloat16 [16, 256, 256], P(('region', 'tile')), parts along dimension 0, may hold values from -1 to 1
- master_mask: bfloat16 [8, 256, 256], P(('region', 'tile')), parts along dimension 0, may hold values from -1 to 1
- target: bfloat16 [16, 256, 256], P(('region', 'tile')), parts along dimension 0, may hold values from 0 to 1
- inst_master: int32 [16], P(('region', 'tile')), parts along dimension 0, may hold values from 0 to 3, as said below
- inst_shift: int32 [16, 2], P(('region', 'tile')), parts along dimension 0, may hold values from 0 to 255
- kernels: float32 [2, 12, 2, 32, 32], P('corner'), may hold values from -24 to 24
- kernel_weight: float32 [2, 12], P('corner'), may hold values from 0.05 to 1
- corner_dose: float32 [2], P('corner'), may hold values from 0.6 to 1.6
Outputs:
- tile_grad: float32 [16, 256, 256], P(('region', 'tile')), parts along dimension 0
- master_grad: float32 [8, 256, 256], P(('region', 'tile')), parts along dimension 0
There are 2 independent parts, one for each index of `region`. A program takes and returns all parts, laid end to end along the dimension named above; an argument that names none is the same for every part. Nothing has to cross between parts.
Inputs may be any that keep to these rules, and one draw needn't show every extreme that they name: `inst_master`: each master cell is placed in exactly 2 tiles.
All inputs are finite; a program needn't handle non-finite values.
Results may differ from a plain program's by a relative error of at most 0.0003.
Values may be sent and summed in bfloat16 or wider, within the bound.
No kernel may reach another device: no remote copies, remote signals or barrier semaphores. Data moves between devices by JAX's collectives and lax.ppermute only.
A program may use at most 64 MiB of HBM per device.

v0:
```python
import math
import numpy as np
import jax
import jax.numpy as jnp
from jax import lax
from jax.sharding import PartitionSpec as P

P_SIZE = 256
B = 32
precise = lax.Precision.HIGHEST
steepness = 3.0
threshold = 1.0


def band_tables():
    freq = np.arange(B, dtype=np.int64) - B // 2
    pixel = np.arange(P_SIZE, dtype=np.int64)
    angle = (
        2.0 * math.pi / P_SIZE * np.mod(freq[:, None] * pixel[None, :], P_SIZE).astype(np.float64)
    )
    return (jnp.asarray(np.cos(angle), jnp.float32), jnp.asarray(-np.sin(angle), jnp.float32))


def phase_ramp(shift):
    freq = jnp.arange(B, dtype=jnp.int32) - B // 2
    total = (
        freq[None, :, None] * shift[:, 0][:, None, None]
        + freq[None, None, :] * shift[:, 1][:, None, None]
    )
    angle = 2.0 * math.pi / P_SIZE * jnp.mod(total, P_SIZE).astype(jnp.float32)
    return (jnp.cos(angle), -jnp.sin(angle))


def spectra(masks, cos_tab, sin_tab):
    rows_re = jnp.einsum("bx,nxy->nby", cos_tab, masks, precision=precise)
    rows_im = jnp.einsum("bx,nxy->nby", sin_tab, masks, precision=precise)
    spec_re = jnp.einsum("nby,cy->nbc", rows_re, cos_tab, precision=precise) - jnp.einsum(
        "nby,cy->nbc", rows_im, sin_tab, precision=precise
    )
    spec_im = jnp.einsum("nby,cy->nbc", rows_re, sin_tab, precision=precise) + jnp.einsum(
        "nby,cy->nbc", rows_im, cos_tab, precision=precise
    )
    return (spec_re, spec_im)


def back_pixels(x_re, x_im, cos_tab, sin_tab):
    half_re = jnp.einsum("bx,nbc->nxc", cos_tab, x_re, precision=precise) + jnp.einsum(
        "bx,nbc->nxc", sin_tab, x_im, precision=precise
    )
    half_im = jnp.einsum("bx,nbc->nxc", cos_tab, x_im, precision=precise) - jnp.einsum(
        "bx,nbc->nxc", sin_tab, x_re, precision=precise
    )
    return jnp.einsum("nxc,cy->nxy", half_re, cos_tab, precision=precise) + jnp.einsum(
        "nxc,cy->nxy", half_im, sin_tab, precision=precise
    )


def on_device(
    tile_mask, master_mask, target, inst_master, inst_shift, kernels, kernel_weight, corner_dose
):
    cos_tab, sin_tab = band_tables()
    scale = 1.0 / (P_SIZE * P_SIZE)
    local_tiles = tile_mask.shape[0]
    local_masters = master_mask.shape[0]
    tile_count = lax.axis_size("tile")
    tile_pos = lax.axis_index("tile")
    kern_count = lax.axis_size("kern")
    kern_pos = lax.axis_index("kern")
    per_dev = local_tiles // kern_count
    first = kern_pos * per_dev
    region_tiles = tile_count * local_tiles
    region_masters = tile_count * local_masters
    with jax.named_scope("master_spectra"):
        own_re, own_im = spectra(master_mask.astype(jnp.float32), cos_tab, sin_tab)
        own = jnp.stack([own_re, own_im], axis=1)
        every = lax.all_gather(own, "tile", axis=0, tiled=True)
    with jax.named_scope("tile_spectra"):
        mine_mask = lax.dynamic_slice_in_dim(tile_mask, first, per_dev, 0)
        goal = lax.dynamic_slice_in_dim(target, first, per_dev, 0).astype(jnp.float32)
        mine_master = lax.dynamic_slice_in_dim(inst_master, first, per_dev, 0)
        mine_shift = lax.dynamic_slice_in_dim(inst_shift, first, per_dev, 0)
        tile_re, tile_im = spectra(mine_mask.astype(jnp.float32), cos_tab, sin_tab)
        ph_re, ph_im = phase_ramp(mine_shift)
        pick = (
            mine_master[:, None] == jnp.arange(region_masters, dtype=jnp.int32)[None, :]
        ).astype(jnp.float32)
        sel = jnp.sum(pick[:, :, None, None, None] * every[None], axis=1)
        sel_re = sel[:, 0]
        sel_im = sel[:, 1]
        spec_re = tile_re + (ph_re * sel_re - ph_im * sel_im)
        spec_im = tile_im + (ph_re * sel_im + ph_im * sel_re)
    dose = corner_dose[0]
    h_re = kernels[0, :, 0]
    h_im = kernels[0, :, 1]
    weights = kernel_weight[0]
    with jax.named_scope("forward_fields"):
        x_re = h_re[:, None] * spec_re[None] - h_im[:, None] * spec_im[None]
        x_im = h_re[:, None] * spec_im[None] + h_im[:, None] * spec_re[None]
        half_re = jnp.einsum("bx,knbc->knxc", cos_tab, x_re, precision=precise) + jnp.einsum(
            "bx,knbc->knxc", sin_tab, x_im, precision=precise
        )
        half_im = jnp.einsum("bx,knbc->knxc", cos_tab, x_im, precision=precise) - jnp.einsum(
            "bx,knbc->knxc", sin_tab, x_re, precision=precise
        )
        f_re = (
            jnp.einsum("knxc,cy->knxy", half_re, cos_tab, precision=precise)
            + jnp.einsum("knxc,cy->knxy", half_im, sin_tab, precision=precise)
        ) * scale
        f_im = (
            jnp.einsum("knxc,cy->knxy", half_im, cos_tab, precision=precise)
            - jnp.einsum("knxc,cy->knxy", half_re, sin_tab, precision=precise)
        ) * scale
    with jax.named_scope("resist_sensitivity"):
        intensity = jnp.sum(weights[:, None, None, None] * (f_re * f_re + f_im * f_im), axis=0)
        resist = jax.nn.sigmoid(steepness * (dose * intensity - threshold))
        sens = 2.0 * (resist - goal) * resist * (1.0 - resist) * steepness * dose
    with jax.named_scope("adjoint_spectra"):
        g_re = (2.0 * weights)[:, None, None, None] * sens[None] * f_re
        g_im = (2.0 * weights)[:, None, None, None] * sens[None] * f_im
        mid_re = jnp.einsum("knxy,cy->knxc", g_re, cos_tab, precision=precise) - jnp.einsum(
            "knxy,cy->knxc", g_im, sin_tab, precision=precise
        )
        mid_im = jnp.einsum("knxy,cy->knxc", g_re, sin_tab, precision=precise) + jnp.einsum(
            "knxy,cy->knxc", g_im, cos_tab, precision=precise
        )
        out_re = (
            jnp.einsum("bx,knxc->knbc", cos_tab, mid_re, precision=precise)
            - jnp.einsum("bx,knxc->knbc", sin_tab, mid_im, precision=precise)
        ) * scale
        out_im = (
            jnp.einsum("bx,knxc->knbc", cos_tab, mid_im, precision=precise)
            + jnp.einsum("bx,knxc->knbc", sin_tab, mid_re, precision=precise)
        ) * scale
        grad_re = jnp.sum(h_re[:, None] * out_re + h_im[:, None] * out_im, axis=0)
        grad_im = jnp.sum(h_re[:, None] * out_im - h_im[:, None] * out_re, axis=0)
    with jax.named_scope("gradient_exchange"):
        back_re = ph_re * grad_re + ph_im * grad_im
        back_im = ph_re * grad_im - ph_im * grad_re
        tile_slot = tile_pos * local_tiles + first + jnp.arange(per_dev, dtype=jnp.int32)
        tile_pick = (
            tile_slot[:, None] == jnp.arange(region_tiles, dtype=jnp.int32)[None, :]
        ).astype(jnp.float32)
        own_grad = jnp.stack([grad_re, grad_im], axis=1)
        own_back = jnp.stack([back_re, back_im], axis=1)
        tile_part = jnp.sum(tile_pick[:, :, None, None, None] * own_grad[:, None], axis=0)
        master_part = jnp.sum(pick[:, :, None, None, None] * own_back[:, None], axis=0)
        slots = jnp.concatenate([tile_part, master_part], axis=0)
        summed = lax.psum(slots, ("tile", "corner", "kern"))
        mine_tiles = lax.dynamic_slice_in_dim(summed, tile_pos * local_tiles, local_tiles, 0)
        mine_masters = lax.dynamic_slice_in_dim(
            summed, region_tiles + tile_pos * local_masters, local_masters, 0
        )
    with jax.named_scope("pixel_gradients"):
        tile_grad = back_pixels(mine_tiles[:, 0], mine_tiles[:, 1], cos_tab, sin_tab)
        master_grad = back_pixels(mine_masters[:, 0], mine_masters[:, 1], cos_tab, sin_tab)
    return (tile_grad, master_grad)


def solution(mesh):
    return jax.shard_map(
        on_device,
        mesh=mesh,
        in_specs=(
            P(("region", "tile"), None, None),
            P(("region", "tile"), None, None),
            P(("region", "tile"), None, None),
            P(("region", "tile")),
            P(("region", "tile"), None),
            P("corner", None, None, None, None),
            P("corner", None),
            P("corner"),
        ),
        out_specs=(P(("region", "tile"), None, None), P(("region", "tile"), None, None)),
        check_vma=False,
    )
```

profile of v0, /device:TPU:0, one launch (start us, length us, event | category | flops | bytes accessed | tf_op | source)
XLA Modules:
  0.0 185.2 jit_solution(1260496238623281663)
XLA Ops:
  7.2 0.0 copy-start
  7.2 0.0 copy-start.6
  7.2 0.0 all-reduce.2.cloned.1.call-start
  7.3 1.1 fusion.41
  8.4 1.1 fusion.39
  9.5 0.9 fusion.81
  10.5 0.9 fusion.80
  11.4 1.0 convolution_bitcast_fusion.1
  12.4 1.0 convolution_bitcast_fusion
  13.3 0.9 fusion.79
  14.3 0.9 fusion.82
  15.2 0.7 constant_dynamic-slice_fusion
  15.9 0.6 fusion.78
  16.5 1.3 dynamic_slice.20
  17.8 0.7 compare_convert_fusion
  18.5 0.9 fusion.26
  19.4 0.9 fusion.27
  20.4 15.1 %all_gather.3 = f32[4,2,32,32]{3,2,1,0:T(8,128)S(1)} all-gather(f32[1,2,32,32]{3,2,1,0:T(8,128)S(1)} %pad_maximum_fusion.1), channel_id=1, replica_groups=mesh['region'=2,'tile'=4,'corner'=2,'kern'=2] {'tile'}, dimensions={0}, use_global_device_ids=true | all-gather | bytes 40960 | tf_op jit(solution)/shard_map/master_spectra/all_gather | solution.py:76
  35.4 1.3 fusion.75
  36.7 0.1 multiply_reduce_fusion.1
  36.8 0.9 fusion.28
  37.7 0.1 copy.17
  37.8 0.9 fusion.25
  38.8 0.1 copy.19
  38.8 1.1 fusion.77
  39.9 0.1 copy.22
  40.0 0.1 copy.23
  40.2 0.4 fusion.47
  40.6 0.5 fusion.51
  41.1 0.5 fusion.14
  41.5 0.5 fusion.15
  42.0 2.7 %fusion.83 = f32[12,256,256]{2,1,0:T(8,128)S(1)} fusion(f32[12,256,32]{1,2,0:T(8,128)S(1)} %fusion.15, f32[32,256,1]{1,0,2:T(8,128)S(1)} %copy-done.6), kind=kOutput, calls=%fused_computation.143 | convolution fusion | flops 301989888 | bytes 3571712 | tf_op jit(solution)/shard_map/forward_fields/knxc,cy->knxy/dot_general | solution.py:106
  44.8 4.3 %fusion.84 = f32[12,256,256]{2,1,0:T(8,128)} fusion(f32[12,256,32]{1,2,0:T(8,128)S(1)} %fusion.14, f32[32,256,1]{1,0,2:T(8,128)S(1)} %copy-done.6), kind=kOutput, calls=%fused_computation.144 | convolution fusion | flops 301989888 | bytes 3571712 | tf_op jit(solution)/shard_map/forward_fields/knxc,cy->knxy/dot_general | solution.py:110
  49.1 2.7 %add_multiply_fusion = f32[12,256,256]{2,1,0:T(8,128)S(1)} fusion(f32[12,256,256]{2,1,0:T(8,128)S(1)} %fusion.83, f32[12,256,32]{1,2,0:T(8,128)S(1)} %fusion.14, f32[32,256,1]{1,0,2:T(8,128)S(1)} %copy-done.5), kind=kOutput, calls=%fused_computation.4 | convolution fusion | flops 303562752 | bytes 6717440 | tf_op jit(solution)/shard_map/forward_fields/knxc,cy->knxy/dot_general | solution.py:107
  52.5 5.6 %multiply_reduce_fusion = (f32[256,256]{1,0:T(8,128)S(1)}, f32[12,256,256]{2,1,0:T(8,128)S(1)}) fusion(f32[12,256,256]{2,1,0:T(8,128)S(1)} %add_multiply_fusion, f32[12]{0:T(128)S(1)} %bitcast.235, f32[12,256,256]{2,1,0:T(8,128)} %fusion.84, f32[12,256,32]{1,2,0:T(8,128)} %copy-done.7, f32[32,256,1]{1,0,2:T(8,128)S(1)} %copy-done.5), kind=kOutput, calls=%fused_computation.2 | convolution fusion | flops 307429376 | bytes 10125360 | tf_op jit(solution)/shard_map/forward_fields/knxc,cy->knxy/dot_general | solution.py:111
  58.1 0.1 fusion.32
  58.3 3.3 %fusion = f32[12,256,32]{1,2,0:T(8,128)S(1)} fusion(f32[32,256,1]{1,0,2:T(8,128)S(1)} %copy-done.5, f32[12,256,256]{2,1,0:T(8,128)S(1)} %add_multiply_fusion, f32[256,256]{1,0:T(8,128)S(1)} %fusion.32, f32[12]{0:T(128)S(1)} %broadcast_multiply_fusion.2), kind=kOutput, calls=%fused_computation.5 | convolution fusion | flops 303562752 | bytes 3833904 | tf_op jit(solution)/shard_map/adjoint_spectra/knxy,cy->knxc/dot_general | solution.py:123
  61.6 3.3 %fusion.1 = f32[12,256,32]{1,2,0:T(8,128)S(1)} fusion(f32[32,256,1]{1,0,2:T(8,128)S(1)} %copy-done.6, f32[12,256,256]{2,1,0:T(8,128)S(1)} %add_multiply_fusion, f32[256,256]{1,0:T(8,128)S(1)} %fusion.32, f32[12]{0:T(128)S(1)} %broadcast_multiply_fusion.2), kind=kOutput, calls=%fused_computation.6 | convolution fusion | flops 303562752 | bytes 3833904 | tf_op jit(solution)/shard_map/adjoint_spectra/knxy,cy->knxc/dot_general | solution.py:120
  64.8 3.3 %fusion.13 = f32[12,256,32]{1,2,0:T(8,128)S(1)} fusion(f32[12,256,32]{1,2,0:T(8,128)S(1)} %fusion, f32[32,256,1]{1,0,2:T(8,128)S(1)} %copy-done.6, f32[12,256,256]{2,1,0:T(8,128)S(1)} %get-tuple-element.11, f32[256,256]{1,0:T(8,128)S(1)} %fusion.32, f32[12]{0:T(128)S(1)} %broadcast_multiply_fusion.2), kind=kOutput, calls=%fused_computation.19 | convolution fusion | flops 303661056 | bytes 4227120 | tf_op jit(solution)/shard_map/adjoint_spectra/knxy,cy->knxc/dot_general | solution.py:123
  68.2 3.5 %fusion.12 = f32[12,256,32]{1,2,0:T(8,128)S(1)} fusion(f32[12,256,32]{1,2,0:T(8,128)S(1)} %fusion.1, f32[32,256,1]{1,0,2:T(8,128)S(1)} %copy-done.5, f32[12,256,256]{2,1,0:T(8,128)S(1)} %get-tuple-element.11, f32[256,256]{1,0:T(8,128)S(1)} %fusion.32, f32[12]{0:T(128)S(1)} %broadcast_multiply_fusion.2), kind=kOutput, calls=%fused_computation.18 | convolution fusion | flops 303661056 | bytes 4227120 | tf_op jit(solution)/shard_map/adjoint_spectra/knxy,cy->knxc/dot_general | solution.py:120
  71.7 0.5 fusion.85
  72.1 0.5 fusion.86
  72.6 0.5 fusion.20
  73.1 0.5 fusion.34
  73.6 0.2 multiply_add_fusion
  73.7 0.1 copy.20
  73.8 0.1 copy.21
  73.9 0.1 broadcast_multiply_fusion.1
  74.0 0.1 broadcast_multiply_fusion
  74.1 0.8 pad_maximum_fusion
  74.9 0.0 all-reduce.2.cloned.1.call-update
  74.9 91.9 %all-reduce.2.cloned.1.call-done = f32[12,2,32,32]{3,2,1,0:T(8,128)} async-done(((f32[12,2,32,32]{3,2,1,0:T(8,128)}), f32[12,2,32,32]{3,2,1,0:T(8,128)}) %all-reduce.2.cloned.1.call-update) | async-done | bytes 98320 | tf_op jit(solution)/shard_map/gradient_exchange/psum | solution.py:148
  166.8 0.9 fusion.61
  167.8 0.9 fusion.24
  168.7 0.4 fusion.88
  169.2 1.0 fusion.53
  170.2 1.0 fusion.22
  171.2 0.6 fusion.87
  171.8 0.9 fusion.62
  172.8 0.9 fusion.23
  173.7 1.1 fusion.16
  174.9 1.0 fusion.54
  175.9 1.0 fusion.21
  176.9 1.4 convolution_add_fusion
  (27 shorter events, 0.1 us)
Async XLA Ops:
  7.2 4.2 %copy-start = (bf16[2,256,256]{2,1,0:T(8,128)(2,1)S(1)}, bf16[2,256,256]{2,1,0:T(8,128)(2,1)}, u32[]{:S(2)}) copy-start(bf16[2,256,256]{2,1,0:T(8,128)(2,1)} %param.10) | copy-start | bytes 786436
  7.2 33.0 %copy-start.6 = (f32[32,256,1]{1,0,2:T(8,128)S(1)}, f32[32,256,1]{1,0,2:T(8,128)}, u32[]{:S(2)}) copy-start(f32[32,256,1]{1,0,2:T(8,128)} %constant.68) | copy-start | bytes 98308
  7.2 33.9 %copy-start.5 = (f32[32,256,1]{1,0,2:T(8,128)S(1)}, f32[32,256,1]{1,0,2:T(8,128)}, u32[]{:S(2)}) copy-start(f32[32,256,1]{1,0,2:T(8,128)} %constant.69) | copy-start | bytes 98308
  7.2 159.6 %all-reduce.2.cloned.1.call-start = ((), (), s32[]{:S(2)}) async-start(), calls=%async_computation | async-start | bytes 786432 | tf_op jit(solution)/shard_map/gradient_exchange/psum | solution.py:148
  40.0 4.8 %copy-start.1 = (f32[1,12,1,32,32]{3,4,1,2,0:T(8,128)}, f32[1,12,1,32,32]{3,4,1,2,0:T(8,128)S(1)}, u32[]{:S(2)}) copy-start(f32[1,12,1,32,32]{3,4,1,2,0:T(8,128)S(1)} %copy.22) | copy-start | bytes 147460
  40.1 4.6 %copy-start.3 = (f32[1,12,1,32,32]{3,4,1,2,0:T(8,128)}, f32[1,12,1,32,32]{3,4,1,2,0:T(8,128)S(1)}, u32[]{:S(2)}) copy-start(f32[1,12,1,32,32]{3,4,1,2,0:T(8,128)S(1)} %copy.23) | copy-start | bytes 147460
  42.0 2.8 %copy-start.7 = (f32[12,256,32]{1,2,0:T(8,128)}, f32[12,256,32]{1,2,0:T(8,128)S(1)}, u32[]{:S(2)}) copy-start(f32[12,256,32]{1,2,0:T(8,128)S(1)} %fusion.15) | copy-start | bytes 1179652
  49.1 3.4 %copy-start.11 = (f32[1,12]{1,0:T(1,128)S(1)}, f32[1,12]{1,0:T(1,128)}, u32[]{:S(2)}) copy-start(f32[1,12]{1,0:T(1,128)} %param.16) | copy-start | bytes 148
  52.5 5.6 %copy-start.10 = (bf16[2,256,256]{2,1,0:T(8,128)(2,1)S(1)}, bf16[2,256,256]{2,1,0:T(8,128)(2,1)}, u32[]{:S(2)}) copy-start(bf16[2,256,256]{2,1,0:T(8,128)(2,1)} %param.12) | copy-start | bytes 786436
  68.1 4.9 %copy-start.2 = (f32[1,12,1,32,32]{3,4,1,2,0:T(8,128)S(1)}, f32[1,12,1,32,32]{3,4,1,2,0:T(8,128)}, u32[]{:S(2)}) copy-start(f32[1,12,1,32,32]{3,4,1,2,0:T(8,128)} %copy-done.1) | copy-start | bytes 147460
  68.1 4.9 %copy-start.4 = (f32[1,12,1,32,32]{3,4,1,2,0:T(8,128)S(1)}, f32[1,12,1,32,32]{3,4,1,2,0:T(8,128)}, u32[]{:S(2)}) copy-start(f32[1,12,1,32,32]{3,4,1,2,0:T(8,128)} %copy-done.3) | copy-start | bytes 147460
  71.6 95.2 %copy-start.9 = (f32[32,256]{1,0:T(8,128)S(1)}, f32[32,256]{1,0:T(8,128)}, u32[]{:S(2)}) copy-start(f32[32,256]{1,0:T(8,128)} %constant.58.clone) | copy-start | bytes 98308
  71.7 96.1 %copy-start.8 = (f32[32,256]{1,0:T(8,128)S(1)}, f32[32,256]{1,0:T(8,128)}, u32[]{:S(2)}) copy-start(f32[32,256]{1,0:T(8,128)} %constant.59.clone) | copy-start | bytes 98308
Sparse Core Ops, SparseCore 0:
  75.0 91.7 all-reduce.1
where the time goes:
time: 187 us; the launch traced here: 185 us
  waiting for transfers between devices  91.9 us (49%)
  matrix products  55.3 us (30%)
  between operations  15.2 us (8%)
  blocking collectives  15.1 us (8%)
  local copies, waits for them, and re-layouts  4.24 us (2%)
  other arithmetic  3.34 us (2%)
    psum x1, waiting for transfers between devices, on_device(): summed = lax.psum(slots, ('tile', 'corner', 'kern'))  91.9 us
    all_gather x1, blocking collectives, on_device(): every = lax.all_gather(own, 'tile', axis=0, tiled=True)  15.1 us
    dot_general x1, matrix products, on_device(): jnp.einsum('knxc,cy->knxy', half_re, sin_tab, precision=precise)  5.58 us
    dot_general x1, matrix products, on_device(): jnp.einsum('knxc,cy->knxy', half_im, cos_tab, precision=precise)  4.34 us
  transfers between devices with their start and end apart: 1, of which 1 were waited for; matrix products, arithmetic and copies ran while one was open for 0% of the time, Pallas kernels for 0%

commit v1 on v0

--- a/solution.py
+++ b/solution.py
@@ -145,7 +145,7 @@
         tile_part = jnp.sum(tile_pick[:, :, None, None, None] * own_grad[:, None], axis=0)
         master_part = jnp.sum(pick[:, :, None, None, None] * own_back[:, None], axis=0)
         slots = jnp.concatenate([tile_part, master_part], axis=0)
-        summed = lax.psum(slots, ("tile", "corner", "kern"))
+        summed = lax.psum(lax.psum(slots, ("corner", "kern")), axis_name="tile")
         mine_tiles = lax.dynamic_slice_in_dim(summed, tile_pos * local_tiles, local_tiles, 0)
         mine_masters = lax.dynamic_slice_in_dim(
             summed, region_tiles + tile_pos * local_masters, local_masters, 0

time: 187 us -> 168 us (0.90)
  waiting for transfers between devices: 91.9 us -> 73.6 us
    psum x1 -> x2, waiting for transfers between devices: 91.9 us -> 73.6 us  [on_device(): summed = lax.psum(lax.psum(slots, ('corner', 'kern')), axis_name='tile')]
  transfers between devices with their start and end apart: 1 -> 2, of which waited for: 1 -> 2; matrix products, arithmetic and copies ran while one was open for 0% -> 0% of each run, Pallas kernels for 0% -> 0%
where the time goes in v1:
time: 168 us; the launch traced here: 167 us
  waiting for transfers between devices  73.6 us (44%)
  matrix products  55.3 us (33%)
  between operations  15.2 us (9%)
  blocking collectives  15.1 us (9%)
  local copies, waits for them, and re-layouts  4.24 us (3%)
  other arithmetic  3.34 us (2%)
    psum x2, waiting for transfers between devices, on_device(): summed = lax.psum(lax.psum(slots, ('corner', 'kern')), axis_name='tile')  73.6 us
    all_gather x1, blocking collectives, on_device(): every = lax.all_gather(own, 'tile', axis=0, tiled=True)  15.1 us
    dot_general x1, matrix products, on_device(): jnp.einsum('knxc,cy->knxy', half_re, sin_tab, precision=precise)  5.58 us
    dot_general x1, matrix products, on_device(): jnp.einsum('knxc,cy->knxy', half_im, cos_tab, precision=precise)  4.34 us
    dot_general x1, matrix products, on_device(): jnp.einsum('knxy,cy->knxc', g_im, sin_tab, precision=precise)  3.49 us
  transfers between devices with their start and end apart: 2, of which 2 were waited for; matrix products, arithmetic and copies ran while one was open for 0% of the time, Pallas kernels for 0%

profile of v1, /device:TPU:0, one launch (start us, length us, event | category | flops | bytes accessed | tf_op | source)
XLA Modules:
  0.0 166.9 jit_solution(4923410638888597739)
XLA Ops:
  7.2 0.0 all-reduce.3.cloned.1.call-start
  7.3 1.1 fusion.41
  8.4 1.1 fusion.39
  9.5 0.9 fusion.81
  10.5 0.9 fusion.80
  11.4 1.0 convolution_bitcast_fusion.1
  12.4 1.0 convolution_bitcast_fusion
  13.3 0.9 fusion.79
  14.3 0.9 fusion.82
  15.2 0.7 constant_dynamic-slice_fusion
  15.9 0.6 fusion.78
  16.5 1.3 dynamic_slice.20
  17.8 0.7 compare_convert_fusion
  18.5 0.9 fusion.26
  19.4 0.9 fusion.27
  20.4 15.1 %all_gather.3 = f32[4,2,32,32]{3,2,1,0:T(8,128)S(1)} all-gather(f32[1,2,32,32]{3,2,1,0:T(8,128)S(1)} %pad_maximum_fusion.1), channel_id=1, replica_groups=mesh['region'=2,'tile'=4,'corner'=2,'kern'=2] {'tile'}, dimensions={0}, use_global_device_ids=true | all-gather | bytes 40960 | tf_op jit(solution)/shard_map/master_spectra/all_gather | solution.py:76
  35.4 1.3 fusion.75
  36.7 0.1 multiply_reduce_fusion.1
  36.8 0.9 fusion.28
  37.7 0.1 copy.17
  37.8 0.9 fusion.25
  38.8 0.1 copy.19
  38.8 1.1 fusion.77
  39.9 0.1 copy.22
  40.0 0.1 copy.23
  40.2 0.4 fusion.47
  40.6 0.5 fusion.51
  41.1 0.5 fusion.14
  41.5 0.5 fusion.15
  42.0 2.7 %fusion.83 = f32[12,256,256]{2,1,0:T(8,128)S(1)} fusion(f32[12,256,32]{1,2,0:T(8,128)S(1)} %fusion.15, f32[32,256,1]{1,0,2:T(8,128)S(1)} %copy-done.6), kind=kOutput, calls=%fused_computation.143 | convolution fusion | flops 301989888 | bytes 3571712 | tf_op jit(solution)/shard_map/forward_fields/knxc,cy->knxy/dot_general | solution.py:106
  44.8 4.3 %fusion.84 = f32[12,256,256]{2,1,0:T(8,128)} fusion(f32[12,256,32]{1,2,0:T(8,128)S(1)} %fusion.14, f32[32,256,1]{1,0,2:T(8,128)S(1)} %copy-done.6), kind=kOutput, calls=%fused_computation.144 | convolution fusion | flops 301989888 | bytes 3571712 | tf_op jit(solution)/shard_map/forward_fields/knxc,cy->knxy/dot_general | solution.py:110
  49.1 2.7 %add_multiply_fusion = f32[12,256,256]{2,1,0:T(8,128)S(1)} fusion(f32[12,256,256]{2,1,0:T(8,128)S(1)} %fusion.83, f32[12,256,32]{1,2,0:T(8,128)S(1)} %fusion.14, f32[32,256,1]{1,0,2:T(8,128)S(1)} %copy-done.5), kind=kOutput, calls=%fused_computation.4 | convolution fusion | flops 303562752 | bytes 6717440 | tf_op jit(solution)/shard_map/forward_fields/knxc,cy->knxy/dot_general | solution.py:107
  52.5 5.6 %multiply_reduce_fusion = (f32[256,256]{1,0:T(8,128)S(1)}, f32[12,256,256]{2,1,0:T(8,128)S(1)}) fusion(f32[12,256,256]{2,1,0:T(8,128)S(1)} %add_multiply_fusion, f32[12]{0:T(128)S(1)} %bitcast.235, f32[12,256,256]{2,1,0:T(8,128)} %fusion.84, f32[12,256,32]{1,2,0:T(8,128)} %copy-done.7, f32[32,256,1]{1,0,2:T(8,128)S(1)} %copy-done.5), kind=kOutput, calls=%fused_computation.2 | convolution fusion | flops 307429376 | bytes 10125360 | tf_op jit(solution)/shard_map/forward_fields/knxc,cy->knxy/dot_general | solution.py:111
  58.1 0.1 fusion.32
  58.3 3.3 %fusion = f32[12,256,32]{1,2,0:T(8,128)S(1)} fusion(f32[32,256,1]{1,0,2:T(8,128)S(1)} %copy-done.5, f32[12,256,256]{2,1,0:T(8,128)S(1)} %add_multiply_fusion, f32[256,256]{1,0:T(8,128)S(1)} %fusion.32, f32[12]{0:T(128)S(1)} %broadcast_multiply_fusion.2), kind=kOutput, calls=%fused_computation.5 | convolution fusion | flops 303562752 | bytes 3833904 | tf_op jit(solution)/shard_map/adjoint_spectra/knxy,cy->knxc/dot_general | solution.py:123
  61.6 3.3 %fusion.1 = f32[12,256,32]{1,2,0:T(8,128)S(1)} fusion(f32[32,256,1]{1,0,2:T(8,128)S(1)} %copy-done.6, f32[12,256,256]{2,1,0:T(8,128)S(1)} %add_multiply_fusion, f32[256,256]{1,0:T(8,128)S(1)} %fusion.32, f32[12]{0:T(128)S(1)} %broadcast_multiply_fusion.2), kind=kOutput, calls=%fused_computation.6 | convolution fusion | flops 303562752 | bytes 3833904 | tf_op jit(solution)/shard_map/adjoint_spectra/knxy,cy->knxc/dot_general | solution.py:120
  64.8 3.3 %fusion.13 = f32[12,256,32]{1,2,0:T(8,128)S(1)} fusion(f32[12,256,32]{1,2,0:T(8,128)S(1)} %fusion, f32[32,256,1]{1,0,2:T(8,128)S(1)} %copy-done.6, f32[12,256,256]{2,1,0:T(8,128)S(1)} %get-tuple-element.11, f32[256,256]{1,0:T(8,128)S(1)} %fusion.32, f32[12]{0:T(128)S(1)} %broadcast_multiply_fusion.2), kind=kOutput, calls=%fused_computation.19 | convolution fusion | flops 303661056 | bytes 4227120 | tf_op jit(solution)/shard_map/adjoint_spectra/knxy,cy->knxc/dot_general | solution.py:123
  68.2 3.5 %fusion.12 = f32[12,256,32]{1,2,0:T(8,128)S(1)} fusion(f32[12,256,32]{1,2,0:T(8,128)S(1)} %fusion.1, f32[32,256,1]{1,0,2:T(8,128)S(1)} %copy-done.5, f32[12,256,256]{2,1,0:T(8,128)S(1)} %get-tuple-element.11, f32[256,256]{1,0:T(8,128)S(1)} %fusion.32, f32[12]{0:T(128)S(1)} %broadcast_multiply_fusion.2), kind=kOutput, calls=%fused_computation.18 | convolution fusion | flops 303661056 | bytes 4227120 | tf_op jit(solution)/shard_map/adjoint_spectra/knxy,cy->knxc/dot_general | solution.py:120
  71.7 0.5 fusion.85
  72.1 0.5 fusion.86
  72.6 0.5 fusion.20
  73.1 0.5 fusion.34
  73.6 0.2 multiply_add_fusion
  73.7 0.1 copy.20
  73.8 0.1 copy.21
  73.9 0.1 broadcast_multiply_fusion.1
  74.0 0.1 broadcast_multiply_fusion
  74.1 0.8 pad_maximum_fusion
  74.9 0.0 all-reduce.3.cloned.1.call-update
  74.9 0.0 all-reduce.5.cloned.1.call-start
  74.9 34.0 %all-reduce.3.cloned.1.call-done = f32[12,2,32,32]{3,2,1,0:T(8,128)} async-done(((f32[12,2,32,32]{3,2,1,0:T(8,128)}), f32[12,2,32,32]{3,2,1,0:T(8,128)}) %all-reduce.3.cloned.1.call-update) | async-done | bytes 98320 | tf_op jit(solution)/shard_map/gradient_exchange/psum | solution.py:148
  109.0 39.5 %all-reduce.5.cloned.1.call-done = f32[12,2,32,32]{3,2,1,0:T(8,128)} async-done(((f32[12,2,32,32]{3,2,1,0:T(8,128)}), f32[12,2,32,32]{3,2,1,0:T(8,128)}) %all-reduce.5.cloned.1.call-update) | async-done | bytes 98320 | tf_op jit(solution)/shard_map/gradient_exchange/psum | solution.py:148
  148.6 0.9 fusion.61
  149.5 0.9 fusion.24
  150.5 0.4 fusion.88
  150.9 1.0 fusion.53
  151.9 1.0 fusion.22
  152.9 0.6 fusion.87
  153.6 0.9 fusion.62
  154.5 0.9 fusion.23
  155.5 1.1 fusion.16
  156.6 1.0 fusion.54
  157.6 1.0 fusion.21
  158.6 1.4 convolution_add_fusion
  (30 shorter events, 0.1 us)
Async XLA Ops:
  7.2 4.2 %copy-start = (bf16[2,256,256]{2,1,0:T(8,128)(2,1)S(1)}, bf16[2,256,256]{2,1,0:T(8,128)(2,1)}, u32[]{:S(2)}) copy-start(bf16[2,256,256]{2,1,0:T(8,128)(2,1)} %param.10) | copy-start | bytes 786436
  7.2 33.0 %copy-start.6 = (f32[32,256,1]{1,0,2:T(8,128)S(1)}, f32[32,256,1]{1,0,2:T(8,128)}, u32[]{:S(2)}) copy-start(f32[32,256,1]{1,0,2:T(8,128)} %constant.68) | copy-start | bytes 98308
  7.2 33.9 %copy-start.5 = (f32[32,256,1]{1,0,2:T(8,128)S(1)}, f32[32,256,1]{1,0,2:T(8,128)}, u32[]{:S(2)}) copy-start(f32[32,256,1]{1,0,2:T(8,128)} %constant.69) | copy-start | bytes 98308
  7.2 101.8 %all-reduce.3.cloned.1.call-start = ((), (), s32[]{:S(2)}) async-start(), calls=%async_computation | async-start | bytes 786432 | tf_op jit(solution)/shard_map/gradient_exchange/psum | solution.py:148
  40.0 4.8 %copy-start.1 = (f32[1,12,1,32,32]{3,4,1,2,0:T(8,128)}, f32[1,12,1,32,32]{3,4,1,2,0:T(8,128)S(1)}, u32[]{:S(2)}) copy-start(f32[1,12,1,32,32]{3,4,1,2,0:T(8,128)S(1)} %copy.22) | copy-start | bytes 147460
  40.1 4.6 %copy-start.3 = (f32[1,12,1,32,32]{3,4,1,2,0:T(8,128)}, f32[1,12,1,32,32]{3,4,1,2,0:T(8,128)S(1)}, u32[]{:S(2)}) copy-start(f32[1,12,1,32,32]{3,4,1,2,0:T(8,128)S(1)} %copy.23) | copy-start | bytes 147460
  42.0 2.8 %copy-start.7 = (f32[12,256,32]{1,2,0:T(8,128)}, f32[12,256,32]{1,2,0:T(8,128)S(1)}, u32[]{:S(2)}) copy-start(f32[12,256,32]{1,2,0:T(8,128)S(1)} %fusion.15) | copy-start | bytes 1179652
  49.1 3.4 %copy-start.11 = (f32[1,12]{1,0:T(1,128)S(1)}, f32[1,12]{1,0:T(1,128)}, u32[]{:S(2)}) copy-start(f32[1,12]{1,0:T(1,128)} %param.16) | copy-start | bytes 148
  52.5 5.6 %copy-start.10 = (bf16[2,256,256]{2,1,0:T(8,128)(2,1)S(1)}, bf16[2,256,256]{2,1,0:T(8,128)(2,1)}, u32[]{:S(2)}) copy-start(bf16[2,256,256]{2,1,0:T(8,128)(2,1)} %param.12) | copy-start | bytes 786436
  68.1 4.9 %copy-start.2 = (f32[1,12,1,32,32]{3,4,1,2,0:T(8,128)S(1)}, f32[1,12,1,32,32]{3,4,1,2,0:T(8,128)}, u32[]{:S(2)}) copy-start(f32[1,12,1,32,32]{3,4,1,2,0:T(8,128)} %copy-done.1) | copy-start | bytes 147460
  68.1 4.9 %copy-start.4 = (f32[1,12,1,32,32]{3,4,1,2,0:T(8,128)S(1)}, f32[1,12,1,32,32]{3,4,1,2,0:T(8,128)}, u32[]{:S(2)}) copy-start(f32[1,12,1,32,32]{3,4,1,2,0:T(8,128)} %copy-done.3) | copy-start | bytes 147460
  71.6 76.9 %copy-start.9 = (f32[32,256]{1,0:T(8,128)S(1)}, f32[32,256]{1,0:T(8,128)}, u32[]{:S(2)}) copy-start(f32[32,256]{1,0:T(8,128)} %constant.58.clone) | copy-start | bytes 98308
  71.7 77.8 %copy-start.8 = (f32[32,256]{1,0:T(8,128)S(1)}, f32[32,256]{1,0:T(8,128)}, u32[]{:S(2)}) copy-start(f32[32,256]{1,0:T(8,128)} %constant.59.clone) | copy-start | bytes 98308
  74.9 73.7 %all-reduce.5.cloned.1.call-start = ((), (), s32[]{:S(2)}) async-start(), calls=%async_computation.1 | async-start | bytes 786432 | tf_op jit(solution)/shard_map/gradient_exchange/psum | solution.py:148
Sparse Core Ops, SparseCore 0:
  75.0 33.9 all-reduce.2
  111.4 37.0 all-reduce.4
